TPU v7x, 512 devices: a whole 4x4x16 slice. The times are simulated.
512 devices in a mesh: seq: 64 (over z, y), tensor: 8 (over x, core).
Axes of the slice: x: 4, y: 4, z: 16, core: 2. Of those that a mesh axis runs over, the one named last changes fastest.
Arguments:
- hidden: bfloat16 [8192, 4096], P('seq', 'tensor')
- norm_gain: bfloat16 [4096], replicated, may hold values from 0.5 to 1.5
- w_query: bfloat16 [4096, 4096], P('seq', 'tensor')
- key_value_weight: bfloat16 [4096, 1024], P('seq')
- w_out: bfloat16 [4096, 4096], P('tensor', 'seq'), may hold values from -0.09375 to 0.09375
- prefix_key_cache: bfloat16 [64, 1024, 1024], P('seq')
- prefix_owner: int32 [64], replicated, may hold values from 0 to 63, each once
- token_counts: int32 [64, 64], P('seq'), may hold values from 0 to 4, as said below
Outputs:
- attn_out: bfloat16 [8192, 4096], P('seq', 'tensor')
- suffix_key_cache: bfloat16 [8192, 1024], P('seq', 'tensor')
Inputs may be any that keep to these rules, and one draw needn't show every extreme that they name: `token_counts`: each row sums to 128; one prefix receives exactly 4 tokens from every sequence index.
All inputs are finite; a program needn't handle non-finite values.
Results may differ from a plain program's by a relative error of at most 0.035.
Values may be sent and summed in bfloat16 or wider, within the bound.
No kernel may reach another device: no remote copies, remote signals or barrier semaphores. Data moves between devices by JAX's collectives and lax.ppermute only.
A program may use at most 64 MiB of HBM per device.

v0:
```python
import jax
import jax.numpy as jnp
from jax import lax
from jax.sharding import PartitionSpec as P

HEAD_DIM = 128
PREFIX_LENGTH = 1024
eps = 1e-06
theta = 5000000.0


def rotate(values, positions):
    half = values.shape[-1] // 2
    frequency = theta ** (-jnp.arange(half, dtype=jnp.float32) * 2.0 / values.shape[-1])
    angle = positions.astype(jnp.float32)[:, None] * frequency[None, :]
    cosine = jnp.cos(angle)[:, None, :]
    sine = jnp.sin(angle)[:, None, :]
    first = values[..., :half]
    second = values[..., half:]
    return jnp.concatenate(
        [first * cosine - second * sine, second * cosine + first * sine], axis=-1
    )


def layout(counts_row, length):
    ends = jnp.cumsum(counts_row)
    starts = ends - counts_row
    places = jnp.arange(length, dtype=jnp.int32)
    member = (places[:, None] >= starts[None, :]) & (places[:, None] < ends[None, :])
    labels = jnp.arange(counts_row.shape[0], dtype=jnp.int32)
    prefix_group = jnp.sum(jnp.where(member, labels[None, :], 0), axis=1)
    offset = places - jnp.sum(jnp.where(member, starts[None, :], 0), axis=1)
    return (starts, prefix_group, offset)


def attend(query_vectors, keys, values, allowed):
    scores = lax.dot_general(
        query_vectors, keys, (((1,), (1,)), ((), ())), preferred_element_type=jnp.float32
    )
    scores = scores * (1.0 / query_vectors.shape[-1] ** 0.5)
    if allowed is not None:
        scores = jnp.where(allowed, scores, -1e30)
    top = jnp.max(scores, axis=1, keepdims=True)
    expo = jnp.exp(scores - top)
    total = jnp.sum(expo, axis=1, keepdims=True)
    weights = (expo / total).astype(jnp.bfloat16)
    result = jnp.dot(weights, values, preferred_element_type=jnp.float32)
    return (result, top[:, 0] + jnp.log(total[:, 0]))


def shards(
    hidden,
    norm_gain,
    w_query,
    key_value_weight,
    w_out,
    prefix_key_cache,
    prefix_owner,
    token_counts,
):
    tensor_index = lax.axis_index("tensor")
    tensor_count = lax.axis_size("tensor")
    seq_count = lax.axis_size("seq")
    length = hidden.shape[0]
    head_size = HEAD_DIM
    whole = lax.all_gather(hidden, "tensor", axis=1, tiled=True)
    wide = whole.astype(jnp.float32)
    normalized_input = (
        wide
        * lax.rsqrt(jnp.mean(wide * wide, axis=1, keepdims=True) + eps)
        * norm_gain.astype(jnp.float32)
    ).astype(jnp.bfloat16)
    width_query = w_query.shape[1]
    full_width = key_value_weight.shape[1]
    heads_dev = width_query // head_size
    kv_heads = full_width // (2 * head_size)
    group_full = heads_dev * tensor_count // kv_heads
    kv_local = max(1, heads_dev // group_full)
    kv_start = tensor_index * heads_dev // group_full
    kv_width = kv_local * 2 * head_size
    kv_piece = lax.dynamic_slice_in_dim(key_value_weight, kv_start * 2 * head_size, kv_width, 1)
    packed = jnp.concatenate([w_query, kv_piece, w_out.T], axis=1)
    gathered = lax.all_gather(packed, "seq", axis=0, tiled=True)
    wq_full = gathered[:, :width_query]
    kv_full = gathered[:, width_query : width_query + kv_width]
    wo_cols = gathered[:, width_query + kv_width :]

    def contract(piece):
        return jnp.dot(normalized_input, piece, preferred_element_type=jnp.float32)

    query_vectors = contract(wq_full)
    key_value_pair = contract(kv_full)
    counts = token_counts[0]
    num_groups = counts.shape[0]
    starts, prefix_group, offset = layout(counts, length)
    positions = PREFIX_LENGTH + offset
    query_vectors = rotate(query_vectors.reshape(length, heads_dev, head_size), positions).astype(
        jnp.bfloat16
    )
    pair_blocks = key_value_pair.reshape(length, kv_local, 2, head_size)
    rotated_keys = rotate(pair_blocks[:, :, 0], positions)
    suffix_mine = jnp.stack([rotated_keys, pair_blocks[:, :, 1]], axis=2).astype(jnp.bfloat16)
    share = full_width // tensor_count
    suffix_flat = suffix_mine.reshape(length, kv_width)
    suffix_part = lax.dynamic_slice_in_dim(
        suffix_flat, tensor_index * share - kv_start * 2 * head_size, share, 1
    )
    suffix_keys = suffix_mine[:, :, 0]
    suffix_values = suffix_mine[:, :, 1]
    cache_all = prefix_key_cache[0].reshape(-1, kv_heads, 2, head_size)
    cache_mine = lax.dynamic_slice_in_dim(cache_all, kv_start, kv_local, 1)
    cache_keys = cache_mine[:, :, 0]
    cache_values = cache_mine[:, :, 1]
    group_width = heads_dev // kv_local
    capacity = 2 * length // seq_count
    labels = jnp.arange(num_groups, dtype=jnp.int32)
    owner_match = prefix_owner[None, :] == jnp.arange(seq_count, dtype=jnp.int32)[:, None]
    owner_start = jnp.sum(jnp.where(owner_match, starts[None, :], 0), axis=1)
    owner_count = jnp.sum(jnp.where(owner_match, counts[None, :], 0), axis=1)
    slots = jnp.arange(capacity, dtype=jnp.int32)
    valid = slots[None, :] < owner_count[:, None]
    source_rows = jnp.where(valid, owner_start[:, None] + slots[None, :], 0)
    flat_query = query_vectors.reshape(length, width_query)
    outgoing = jnp.where(valid[:, :, None], flat_query[source_rows], jnp.zeros((), jnp.bfloat16))
    arrived = lax.all_to_all(outgoing, "seq", split_axis=0, concat_axis=0, tiled=True)
    items = arrived.shape[1]
    rows_in = arrived.reshape(seq_count * items, heads_dev, head_size)
    outs = []
    logs = []
    for serve_head in range(heads_dev):
        serve_result, serve_logsum = attend(
            rows_in[:, serve_head],
            cache_keys[:, serve_head // group_width],
            cache_values[:, serve_head // group_width],
            None,
        )
        outs.append(serve_result)
        logs.append(serve_logsum)
    out_block = jnp.stack(outs, axis=1).astype(jnp.bfloat16).reshape(seq_count, items, width_query)
    log_block = jnp.stack(logs, axis=1).reshape(seq_count, items, heads_dev)
    prefix_out = lax.all_to_all(out_block, "seq", split_axis=0, concat_axis=0, tiled=True)
    prefix_log = lax.all_to_all(
        log_block.astype(jnp.bfloat16), "seq", split_axis=0, concat_axis=0, tiled=True
    ).astype(log_block.dtype)
    owner_of_token = jnp.sum(
        jnp.where(prefix_group[:, None] == labels[None, :], prefix_owner[None, :], 0), axis=1
    )
    back_rows = owner_of_token * capacity + offset
    prefix_rows = prefix_out.reshape(seq_count * capacity, heads_dev, head_size)[back_rows]
    prefix_logsum = prefix_log.reshape(seq_count * capacity, heads_dev)[back_rows]
    places = jnp.arange(length, dtype=jnp.int32)
    allowed = (prefix_group[:, None] == prefix_group[None, :]) & (
        places[None, :] <= places[:, None]
    )
    outs = []
    logs = []
    for head in range(heads_dev):
        result, logsum = attend(
            query_vectors[:, head],
            suffix_keys[:, head // group_width],
            suffix_values[:, head // group_width],
            allowed,
        )
        outs.append(result)
        logs.append(logsum)
    suffix_attn = jnp.stack(outs, axis=1)
    suffix_logsum = jnp.stack(logs, axis=1)
    upper = jnp.maximum(prefix_logsum, suffix_logsum)
    left = jnp.exp(prefix_logsum - upper)[..., None]
    right = jnp.exp(suffix_logsum - upper)[..., None]
    context = (
        (left * prefix_rows.astype(jnp.float32) + right * suffix_attn) / (left + right)
    ).astype(jnp.bfloat16)
    context = context.reshape(length, width_query)
    partial_out = lax.dot_general(
        context, wo_cols, (((1,), (1,)), ((), ())), preferred_element_type=jnp.float32
    )
    attn_out = lax.psum_scatter(
        partial_out.astype(jnp.bfloat16), "tensor", scatter_dimension=1, tiled=True
    )
    return (attn_out, suffix_part)


def solution(mesh):
    in_specs = (
        P("seq", "tensor"),
        P(),
        P("seq", "tensor"),
        P("seq", None),
        P("tensor", "seq"),
        P("seq", None, None),
        P(),
        P("seq", None),
    )
    out_specs = (P("seq", "tensor"), P("seq", "tensor"))
    return jax.shard_map(shards, mesh=mesh, in_specs=in_specs, out_specs=out_specs, check_vma=False)
```

profile of v0, /device:TPU:8, one launch (start us, length us, event | category | flops | bytes accessed | tf_op | source)
XLA Modules:
  0.0 344.0 jit_solution(9256899727202618528)
XLA Ops:
  8.1 1.5 pad_maximum_fusion.1
  12.0 0.8 select_reduce_fusion.4
  13.0 2.9 copy.121
  16.6 1.0 multiply_cosine_fusion.1
  17.5 28.1 %all-gather.3.cloned.1.call-done = bf16[128,4096]{1,0:T(8,128)(2,1)} async-done(((bf16[128,512]{1,0:T(8,128)(2,1)}), bf16[128,4096]{1,0:T(8,128)(2,1)}) %all-gather.3.cloned.1.call-update) | async-done | bytes 1048592 | tf_op jit(solution)/shard_map/all_gather | solution.py:66
  45.6 1.5 fusion.3
  47.1 163.3 %all-gather.5.cloned.1.call-done = bf16[4096,1280]{1,0:T(8,128)(2,1)} async-done(((bf16[64,1280]{1,0:T(8,128)(2,1)}), bf16[4096,1280]{1,0:T(8,128)(2,1)}) %all-gather.5.cloned.1.call-update) | async-done | bytes 10485776 | tf_op jit(solution)/shard_map/all_gather | solution.py:83
  210.5 4.0 %fusion.1 = f32[128,512]{1,0:T(8,128)} fusion(bf16[4096,1280]{1,0:T(8,128)(2,1)} %all-gather.5.cloned.1.call-done, bf16[128,4096]{1,0:T(8,128)(2,1)} %all-gather.3.cloned.1.call-done, f32[4096]{0:T(1024)S(1)} %convert_element_type.81, f32[128]{0:T(128)S(1)} %add_rsqrt_fusion), kind=kOutput, calls=%fused_computation.5 | convolution fusion | flops 538968064 | bytes 5521920 | tf_op jit(solution)/shard_map/dot_general | solution.py:89
  214.5 1.0 reshape.627
  215.6 2.8 fusion.6
  218.3 1.0 reshape.633
  219.4 1.0 fusion.29
  220.6 0.9 multiply_subtract_fusion
  222.0 1.2 gather_fusion
  223.2 0.9 broadcast_select_fusion
  224.1 10.2 %all-to-all-start = ((bf16[64,4,512]{2,1,0:T(4,128)(2,1)}), bf16[64,4,512]{2,1,0:T(4,128)(2,1)S(1)}, u32[]{:S(2)}, u32[]{:S(2)}) async-start(bf16[64,4,512]{2,1,0:T(4,128)(2,1)} %broadcast_select_fusion), calls=%async_computation | async-start | bytes 524288 | tf_op jit(solution)/shard_map/all_to_all | solution.py:125
  235.3 16.7 %all-to-all-done = bf16[64,4,512]{2,1,0:T(4,128)(2,1)S(1)} async-done(((bf16[64,4,512]{2,1,0:T(4,128)(2,1)}), bf16[64,4,512]{2,1,0:T(4,128)(2,1)S(1)}, u32[]{:S(2)}, u32[]{:S(2)}) %all-to-all-start) | async-done | bytes 262176 | tf_op jit(solution)/shard_map/all_to_all | solution.py:125
  258.0 5.4 %all-to-all-start.1 = ((bf16[64,4,4]{1,2,0:T(4,128)(2,1)}), bf16[64,4,4]{1,2,0:T(4,128)(2,1)S(1)}, u32[]{:S(2)}, u32[]{:S(2)}) async-start(bf16[64,4,4]{1,2,0:T(4,128)(2,1)} %copy.123), calls=%async_computation.1 | async-start | bytes 131072 | tf_op jit(solution)/shard_map/all_to_all | solution.py:142
  263.7 0.8 convert_element_type.91
  264.6 13.0 %all-to-all-done.1 = bf16[64,4,4]{1,2,0:T(4,128)(2,1)S(1)} async-done(((bf16[64,4,4]{1,2,0:T(4,128)(2,1)}), bf16[64,4,4]{1,2,0:T(4,128)(2,1)S(1)}, u32[]{:S(2)}, u32[]{:S(2)}) %all-to-all-start.1) | async-done | bytes 2080 | tf_op jit(solution)/shard_map/all_to_all | solution.py:142
  277.6 5.5 %all-to-all-start.2 = ((bf16[64,4,512]{2,1,0:T(4,128)(2,1)}), bf16[64,4,512]{2,1,0:T(4,128)(2,1)S(1)}, u32[]{:S(2)}, u32[]{:S(2)}) async-start(bf16[64,4,512]{2,1,0:T(4,128)(2,1)} %convert_element_type.91), calls=%async_computation.2 | async-start | bytes 524288 | tf_op jit(solution)/shard_map/all_to_all | solution.py:141
  284.7 16.4 %all-to-all-done.2 = bf16[64,4,512]{2,1,0:T(4,128)(2,1)S(1)} async-done(((bf16[64,4,512]{2,1,0:T(4,128)(2,1)}), bf16[64,4,512]{2,1,0:T(4,128)(2,1)S(1)}, u32[]{:S(2)}, u32[]{:S(2)}) %all-to-all-start.2) | async-done | bytes 262176 | tf_op jit(solution)/shard_map/all_to_all | solution.py:141
  302.2 4.7 %convolution_convert_fusion = bf16[128,4096]{1,0:T(8,128)(2,1)} fusion(bf16[128,512]{0,1:T(8,128)(2,1)S(1)} %bitcast.161, bf16[4096,1280]{1,0:T(8,128)(2,1)} %all-gather.5.cloned.1.call-done), kind=kOutput, calls=%fused_computation.3 | convolution fusion | flops 537395200 | bytes 5373952 | tf_op jit(solution)/shard_map/dot_general | solution.py:175
  307.7 29.7 %reduce-scatter.2.cloned.1.call-done = bf16[128,512]{1,0:T(8,128)(2,1)} async-done(((bf16[128,4096]{1,0:T(8,128)(2,1)}), bf16[128,512]{1,0:T(8,128)(2,1)}) %reduce-scatter.2.cloned.1.call-update) | async-done | bytes 131088 | tf_op jit(solution)/shard_map/reduce_scatter | solution.py:178
  (100 shorter events, 15.5 us)
Async XLA Ops:
  7.2 0.9 copy-start
  7.2 38.4 %all-gather.3.cloned.1.call-start = ((), (), s32[]{:S(2)}) async-start(), calls=%async_computation.4 | async-start | bytes 1179648 | tf_op jit(solution)/shard_map/all_gather | solution.py:66
  7.9 202.5 %all-gather.5.cloned.1.call-start = ((), (), s32[]{:S(2)}) async-start(), calls=%async_computation.5 | async-start | bytes 10649600 | tf_op jit(solution)/shard_map/all_gather | solution.py:83
  10.3 200.1 %copy-start.2 = (f32[4096]{0:T(1024)}, f32[4096]{0:T(1024)S(1)}, u32[]{:S(2)}) copy-start(f32[4096]{0:T(1024)S(1)} %convert_element_type.81) | copy-start | bytes 49156
  13.0 3.0 copy-start.5
  15.9 194.6 %copy-start.3 = (f32[64]{0:T(128)}, f32[64]{0:T(128)S(1)}, u32[]{:S(2)}) copy-start(f32[64]{0:T(128)S(1)} %multiply_power_fusion) | copy-start | bytes 772
  16.0 0.6 copy-start.6
  16.1 194.3 %copy-start.4 = (f32[128]{0:T(128)}, f32[128]{0:T(128)S(1)}, u32[]{:S(2)}) copy-start(f32[128]{0:T(128)S(1)} %add_convert_fusion.4) | copy-start | bytes 1540
  47.1 163.4 %copy-start.8 = (f32[128]{0:T(128)}, f32[128]{0:T(128)S(1)}, u32[]{:S(2)}) copy-start(f32[128]{0:T(128)S(1)} %add_rsqrt_fusion) | copy-start | bytes 1540
  47.1 168.4 %copy-start.1 = (bf16[128,4096]{1,0:T(8,128)(2,1)S(1)}, bf16[128,4096]{1,0:T(8,128)(2,1)}, u32[]{:S(2)}) copy-start(bf16[128,4096]{1,0:T(8,128)(2,1)} %all-gather.3.cloned.1.call-done) | copy-start | bytes 3145732
  218.3 3.5 %copy-start.7 = (s32[128]{0:T(128)S(1)}, s32[128]{0:T(128)}, u32[]{:S(2)}) copy-start(s32[128]{0:T(128)} %copy-done.6) | copy-start | bytes 1540
  224.1 27.9 %all-to-all-start = ((bf16[64,4,512]{2,1,0:T(4,128)(2,1)}), bf16[64,4,512]{2,1,0:T(4,128)(2,1)S(1)}, u32[]{:S(2)}, u32[]{:S(2)}) async-start(bf16[64,4,512]{2,1,0:T(4,128)(2,1)} %broadcast_select_fusion), calls=%async_computation | async-start | bytes 524288 | tf_op jit(solution)/shard_map/all_to_all | solution.py:125
  258.0 19.6 %all-to-all-start.1 = ((bf16[64,4,4]{1,2,0:T(4,128)(2,1)}), bf16[64,4,4]{1,2,0:T(4,128)(2,1)S(1)}, u32[]{:S(2)}, u32[]{:S(2)}) async-start(bf16[64,4,4]{1,2,0:T(4,128)(2,1)} %copy.123), calls=%async_computation.1 | async-start | bytes 131072 | tf_op jit(solution)/shard_map/all_to_all | solution.py:142
  277.6 23.5 %all-to-all-start.2 = ((bf16[64,4,512]{2,1,0:T(4,128)(2,1)}), bf16[64,4,512]{2,1,0:T(4,128)(2,1)S(1)}, u32[]{:S(2)}, u32[]{:S(2)}) async-start(bf16[64,4,512]{2,1,0:T(4,128)(2,1)} %convert_element_type.91), calls=%async_computation.2 | async-start | bytes 524288 | tf_op jit(solution)/shard_map/all_to_all | solution.py:141
  283.1 54.3 %reduce-scatter.2.cloned.1.call-start = ((), (), s32[]{:S(2)}) async-start(), calls=%async_computation.6 | async-start | bytes 1179648 | tf_op jit(solution)/shard_map/reduce_scatter | solution.py:178
Sparse Core Ops, SparseCore 0:
  10.1 35.3 all-gather.2
  48.5 161.8 all-gather.4
  307.0 30.4 reduce-scatter.1
where the time goes:
time: 345 us; the launch traced here: 344 us
  waiting for transfers between devices  268 us (78%)
  starting transfers between devices  21.3 us (6%)
  matrix products  16 us (5%)
  between operations  14.2 us (4%)
  local copies, waits for them, and re-layouts  13.2 us (4%)
  other arithmetic  11.4 us (3%)
    all_gather x1, waiting for transfers between devices, shards(): gathered = lax.all_gather(packed, 'seq', axis=0, tiled=True)  163 us
    reduce_scatter x1, waiting for transfers between devices, shards(): lax.psum_scatter(partial_out.astype(jnp.bfloat16), 'tensor', scatter_dime...  29.7 us
    all_gather x1, waiting for transfers between devices, shards(): whole = lax.all_gather(hidden, 'tensor', axis=1, tiled=True)  28.1 us
    all_to_all x1, waiting for transfers between devices, shards(): lax.all_to_all(outgoing, 'seq', split_axis=0, concat_axis=0, tiled=True)  16.7 us
    all_to_all x1, waiting for transfers between devices, shards(): lax.all_to_all(out_block, 'seq', split_axis=0, concat_axis=0, tiled=True)  16.4 us
    all_to_all x1, waiting for transfers between devices, shards(): lax.all_to_all(log_block.astype(jnp.bfloat16), 'seq', split_axis=0, conca...  13 us
    all_to_all x1, starting transfers between devices, shards(): lax.all_to_all(outgoing, 'seq', split_axis=0, concat_axis=0, tiled=True)  10.2 us
  transfers between devices with their start and end apart: 6, of which 6 were waited for; matrix products, arithmetic and copies ran while one was open for 4% of the time, Pallas kernels for 0%

commit v1 on v0

--- a/solution.py
+++ b/solution.py
@@ -63,7 +63,14 @@
     seq_count = lax.axis_size("seq")
     length = hidden.shape[0]
     head_size = HEAD_DIM
-    whole = lax.all_gather(hidden, "tensor", axis=1, tiled=True)
+    ring = [hidden]
+    for hop in range(7):
+        ring.append(lax.ppermute(ring[-1], "tensor", [(dev, (dev + 1) % 8) for dev in range(8)]))
+    whole = jnp.roll(
+        jnp.concatenate(ring[::-1], axis=1),
+        (lax.axis_index("tensor") + 1) * ring[0].shape[1],
+        axis=1,
+    )
     wide = whole.astype(jnp.float32)
     normalized_input = (
         wide

time: 345 us -> 307 us (0.89)
  waiting for transfers between devices: 268 us -> 234 us
    all_gather x1, waiting for transfers between devices: 163 us -> 126 us  [shards(): gathered = lax.all_gather(packed, 'seq', axis=0, tiled=True)]
    ppermute x0 -> x7, waiting for transfers between devices: none -> 31.9 us  [shards(): lax.ppermute(ring[-1], 'tensor', [(dev, (dev + 1) % 8) for dev in range(8)])]
    all_gather x1 -> x0, waiting for transfers between devices: 28.1 us -> none  [shards(): whole = lax.all_gather(hidden, 'tensor', axis=1, tiled=True)]
  transfers between devices with their start and end apart: 6 -> 12, of which waited for: 6 -> 12; matrix products, arithmetic and copies ran while one was open for 4% -> 4% of each run, Pallas kernels for 0% -> 0%
where the time goes in v1:
time: 307 us
  waiting for transfers between devices  234 us (76%)
  starting transfers between devices  21.4 us (7%)
  matrix products  14.9 us (5%)
  between operations  14.6 us (5%)
  local copies, waits for them, and re-layouts  13.2 us (4%)
  other arithmetic  8.66 us (3%)
    all_gather x1, waiting for transfers between devices, shards(): gathered = lax.all_gather(packed, 'seq', axis=0, tiled=True)  126 us
    ppermute x7, waiting for transfers between devices, shards(): lax.ppermute(ring[-1], 'tensor', [(dev, (dev + 1) % 8) for dev in range(8)])  31.9 us
    reduce_scatter x1, waiting for transfers between devices, shards(): lax.psum_scatter(partial_out.astype(jnp.bfloat16), 'tensor', scatter_dime...  29.7 us
    all_to_all x1, waiting for transfers between devices, shards(): lax.all_to_all(outgoing, 'seq', split_axis=0, concat_axis=0, tiled=True)  16.7 us
    all_to_all x1, waiting for transfers between devices, shards(): lax.all_to_all(out_block, 'seq', split_axis=0, concat_axis=0, tiled=True)  16.4 us
    all_to_all x1, waiting for transfers between devices, shards(): lax.all_to_all(log_block.astype(jnp.bfloat16), 'seq', split_axis=0, conca...  13 us
    all_to_all x1, starting transfers between devices, shards(): lax.all_to_all(outgoing, 'seq', split_axis=0, concat_axis=0, tiled=True)  10.1 us
  transfers between devices with their start and end apart: 12, of which 12 were waited for; matrix products, arithmetic and copies ran while one was open for 4% of the time, Pallas kernels for 0%

profile of v1, /device:TPU:8, one launch (start us, length us, event | category | flops | bytes accessed | tf_op | source)
XLA Modules:
  0.0 306.7 jit_solution(10967625061668797095)
XLA Ops:
  7.2 0.8 copy-done
  8.1 1.6 pad_maximum_fusion.1
  11.4 4.1 %collective-permute-done = bf16[128,512]{1,0:T(8,128)(2,1)S(1)} collective-permute-done((bf16[128,512]{1,0:T(8,128)(2,1)}, bf16[128,512]{1,0:T(8,128)(2,1)S(1)}, u32[]{:S(2)}, u32[]{:S(2)}) %collective-permute-start) | collective-permute-done | bytes 131104 | tf_op jit(solution)/shard_map/ppermute | solution.py:68
  15.5 5.6 %collective-permute-done.1 = bf16[128,512]{1,0:T(8,128)(2,1)S(1)} collective-permute-done((bf16[128,512]{1,0:T(8,128)(2,1)S(1)}, bf16[128,512]{1,0:T(8,128)(2,1)S(1)}, u32[]{:S(2)}, u32[]{:S(2)}) %collective-permute-start.1) | collective-permute-done | bytes 131104 | tf_op jit(solution)/shard_map/ppermute | solution.py:68
  22.2 4.5 %collective-permute-done.2 = bf16[128,512]{1,0:T(8,128)(2,1)S(1)} collective-permute-done((bf16[128,512]{1,0:T(8,128)(2,1)S(1)}, bf16[128,512]{1,0:T(8,128)(2,1)S(1)}, u32[]{:S(2)}, u32[]{:S(2)}) %collective-permute-start.2) | collective-permute-done | bytes 131104 | tf_op jit(solution)/shard_map/ppermute | solution.py:68
  26.8 5.5 %collective-permute-done.3 = bf16[128,512]{1,0:T(8,128)(2,1)S(1)} collective-permute-done((bf16[128,512]{1,0:T(8,128)(2,1)S(1)}, bf16[128,512]{1,0:T(8,128)(2,1)S(1)}, u32[]{:S(2)}, u32[]{:S(2)}) %collective-permute-start.3) | collective-permute-done | bytes 131104 | tf_op jit(solution)/shard_map/ppermute | solution.py:68
  33.2 4.7 %collective-permute-done.4 = bf16[128,512]{1,0:T(8,128)(2,1)S(1)} collective-permute-done((bf16[128,512]{1,0:T(8,128)(2,1)S(1)}, bf16[128,512]{1,0:T(8,128)(2,1)S(1)}, u32[]{:S(2)}, u32[]{:S(2)}) %collective-permute-start.4) | collective-permute-done | bytes 131104 | tf_op jit(solution)/shard_map/ppermute | solution.py:68
  37.9 5.6 %collective-permute-done.5 = bf16[128,512]{1,0:T(8,128)(2,1)S(1)} collective-permute-done((bf16[128,512]{1,0:T(8,128)(2,1)S(1)}, bf16[128,512]{1,0:T(8,128)(2,1)S(1)}, u32[]{:S(2)}, u32[]{:S(2)}) %collective-permute-start.5) | collective-permute-done | bytes 131104 | tf_op jit(solution)/shard_map/ppermute | solution.py:68
  44.2 2.9 copy.121
  47.2 1.9 collective-permute-done.6
  49.4 1.3 copy-done.1
  51.0 126.1 %all-gather.2.cloned.1.call-done = bf16[4096,1280]{1,0:T(8,128)(2,1)} async-done(((bf16[64,1280]{1,0:T(8,128)(2,1)}), bf16[4096,1280]{1,0:T(8,128)(2,1)}) %all-gather.2.cloned.1.call-update) | async-done | bytes 10485776 | tf_op jit(solution)/shard_map/all_gather | solution.py:90
  177.1 2.4 fusion.6
  180.0 3.3 %fusion.1 = f32[128,512]{1,0:T(8,128)S(1)} fusion(bf16[4096,1280]{1,0:T(8,128)(2,1)} %all-gather.2.cloned.1.call-done, f32[4096]{0:T(1024)S(1)} %convert_element_type.81, f32[128]{0:T(128)S(1)} %add_rsqrt_fusion, bf16[128,8192]{1,0:T(8,128)(2,1)} %copy-done.1, s32[]{:T(128)S(6)} %select_n.94), kind=kOutput, calls=%fused_computation.5 | convolution fusion | flops 538968064 | bytes 5521924 | tf_op jit(solution)/shard_map/dot_general | solution.py:96
  184.2 1.2 gather_fusion
  185.4 0.9 broadcast_select_fusion
  186.3 10.1 %all-to-all-start = ((bf16[64,4,512]{2,1,0:T(4,128)(2,1)}), bf16[64,4,512]{2,1,0:T(4,128)(2,1)S(1)}, u32[]{:S(2)}, u32[]{:S(2)}) async-start(bf16[64,4,512]{2,1,0:T(4,128)(2,1)} %broadcast_select_fusion), calls=%async_computation | async-start | bytes 524288 | tf_op jit(solution)/shard_map/all_to_all | solution.py:132
  197.5 16.7 %all-to-all-done = bf16[64,4,512]{2,1,0:T(4,128)(2,1)S(1)} async-done(((bf16[64,4,512]{2,1,0:T(4,128)(2,1)}), bf16[64,4,512]{2,1,0:T(4,128)(2,1)S(1)}, u32[]{:S(2)}, u32[]{:S(2)}) %all-to-all-start) | async-done | bytes 262176 | tf_op jit(solution)/shard_map/all_to_all | solution.py:132
  220.2 5.4 %all-to-all-start.1 = ((bf16[64,4,4]{1,2,0:T(4,128)(2,1)}), bf16[64,4,4]{1,2,0:T(4,128)(2,1)S(1)}, u32[]{:S(2)}, u32[]{:S(2)}) async-start(bf16[64,4,4]{1,2,0:T(4,128)(2,1)} %copy.123), calls=%async_computation.1 | async-start | bytes 131072 | tf_op jit(solution)/shard_map/all_to_all | solution.py:149
  226.8 13.0 %all-to-all-done.1 = bf16[64,4,4]{1,2,0:T(4,128)(2,1)S(1)} async-done(((bf16[64,4,4]{1,2,0:T(4,128)(2,1)}), bf16[64,4,4]{1,2,0:T(4,128)(2,1)S(1)}, u32[]{:S(2)}, u32[]{:S(2)}) %all-to-all-start.1) | async-done | bytes 2080 | tf_op jit(solution)/shard_map/all_to_all | solution.py:149
  239.8 5.7 %all-to-all-start.2 = ((bf16[64,4,512]{2,1,0:T(4,128)(2,1)}), bf16[64,4,512]{2,1,0:T(4,128)(2,1)S(1)}, u32[]{:S(2)}, u32[]{:S(2)}) async-start(bf16[64,4,512]{2,1,0:T(4,128)(2,1)} %convert_element_type.91), calls=%async_computation.2 | async-start | bytes 524288 | tf_op jit(solution)/shard_map/all_to_all | solution.py:148
  247.1 16.4 %all-to-all-done.2 = bf16[64,4,512]{2,1,0:T(4,128)(2,1)S(1)} async-done(((bf16[64,4,512]{2,1,0:T(4,128)(2,1)}), bf16[64,4,512]{2,1,0:T(4,128)(2,1)S(1)}, u32[]{:S(2)}, u32[]{:S(2)}) %all-to-all-start.2) | async-done | bytes 262176 | tf_op jit(solution)/shard_map/all_to_all | solution.py:148
  264.6 4.7 %convolution_convert_fusion = bf16[128,4096]{1,0:T(8,128)(2,1)} fusion(bf16[128,512]{0,1:T(8,128)(2,1)S(1)} %bitcast.161, bf16[4096,1280]{1,0:T(8,128)(2,1)} %all-gather.2.cloned.1.call-done), kind=kOutput, calls=%fused_computation.3 | convolution fusion | flops 537395200 | bytes 5373952 | tf_op jit(solution)/shard_map/dot_general | solution.py:182
  270.1 29.7 %reduce-scatter.2.cloned.1.call-done = bf16[128,512]{1,0:T(8,128)(2,1)} async-done(((bf16[128,4096]{1,0:T(8,128)(2,1)}), bf16[128,512]{1,0:T(8,128)(2,1)}) %reduce-scatter.2.cloned.1.call-update) | async-done | bytes 131088 | tf_op jit(solution)/shard_map/reduce_scatter | solution.py:185
  (115 shorter events, 18.0 us)
Async XLA Ops:
  7.2 0.9 copy-start
  7.2 170.0 %all-gather.2.cloned.1.call-start = ((), (), s32[]{:S(2)}) async-start(), calls=%async_computation.4 | async-start | bytes 10649600 | tf_op jit(solution)/shard_map/all_gather | solution.py:90
  9.7 5.8 %collective-permute-start = (bf16[128,512]{1,0:T(8,128)(2,1)}, bf16[128,512]{1,0:T(8,128)(2,1)S(1)}, u32[]{:S(2)}, u32[]{:S(2)}) collective-permute-start(bf16[128,512]{1,0:T(8,128)(2,1)} %param.8), channel_id=1, source_target_pairs={{0,1},{1,2},{2,3},{3,4},{4,5},{5,6},{6,7},{7,0},{8,9},{9,10},{10,1... | collective-permute-start | bytes 393224 | tf_op jit(solution)/shard_map/ppermute | solution.py:68
  15.5 5.6 %collective-permute-start.1 = (bf16[128,512]{1,0:T(8,128)(2,1)S(1)}, bf16[128,512]{1,0:T(8,128)(2,1)S(1)}, u32[]{:S(2)}, u32[]{:S(2)}) collective-permute-start(bf16[128,512]{1,0:T(8,128)(2,1)S(1)} %collective-permute-done), channel_id=1, source_target_pairs={{0,1},{1,2},{2,3},{3,4},{4,5},{5,6},{6,7},{7,0},{8,9},{9,10},{10,1... | collective-permute-start | bytes 393224 | tf_op jit(solution)/shard_map/ppermute | solution.py:68
  21.1 5.6 %collective-permute-start.2 = (bf16[128,512]{1,0:T(8,128)(2,1)S(1)}, bf16[128,512]{1,0:T(8,128)(2,1)S(1)}, u32[]{:S(2)}, u32[]{:S(2)}) collective-permute-start(bf16[128,512]{1,0:T(8,128)(2,1)S(1)} %collective-permute-done.1), channel_id=1, source_target_pairs={{0,1},{1,2},{2,3},{3,4},{4,5},{5,6},{6,7},{7,0},{8,9},{9,10},{10,1... | collective-permute-start | bytes 393224 | tf_op jit(solution)/shard_map/ppermute | solution.py:68
  26.7 5.6 %collective-permute-start.3 = (bf16[128,512]{1,0:T(8,128)(2,1)S(1)}, bf16[128,512]{1,0:T(8,128)(2,1)S(1)}, u32[]{:S(2)}, u32[]{:S(2)}) collective-permute-start(bf16[128,512]{1,0:T(8,128)(2,1)S(1)} %collective-permute-done.2), channel_id=1, source_target_pairs={{0,1},{1,2},{2,3},{3,4},{4,5},{5,6},{6,7},{7,0},{8,9},{9,10},{10,1... | collective-permute-start | bytes 393224 | tf_op jit(solution)/shard_map/ppermute | solution.py:68
  32.3 5.6 %collective-permute-start.4 = (bf16[128,512]{1,0:T(8,128)(2,1)S(1)}, bf16[128,512]{1,0:T(8,128)(2,1)S(1)}, u32[]{:S(2)}, u32[]{:S(2)}) collective-permute-start(bf16[128,512]{1,0:T(8,128)(2,1)S(1)} %collective-permute-done.3), channel_id=1, source_target_pairs={{0,1},{1,2},{2,3},{3,4},{4,5},{5,6},{6,7},{7,0},{8,9},{9,10},{10,1... | collective-permute-start | bytes 393224 | tf_op jit(solution)/shard_map/ppermute | solution.py:68
  37.9 5.6 %collective-permute-start.5 = (bf16[128,512]{1,0:T(8,128)(2,1)S(1)}, bf16[128,512]{1,0:T(8,128)(2,1)S(1)}, u32[]{:S(2)}, u32[]{:S(2)}) collective-permute-start(bf16[128,512]{1,0:T(8,128)(2,1)S(1)} %collective-permute-done.4), channel_id=1, source_target_pairs={{0,1},{1,2},{2,3},{3,4},{4,5},{5,6},{6,7},{7,0},{8,9},{9,10},{10,1... | collective-permute-start | bytes 393224 | tf_op jit(solution)/shard_map/ppermute | solution.py:68
  43.5 5.6 %collective-permute-start.6 = (bf16[128,512]{1,0:T(8,128)(2,1)S(1)}, bf16[128,512]{1,0:T(8,128)(2,1)S(1)}, u32[]{:S(2)}, u32[]{:S(2)}) collective-permute-start(bf16[128,512]{1,0:T(8,128)(2,1)S(1)} %collective-permute-done.5), channel_id=1, source_target_pairs={{0,1},{1,2},{2,3},{3,4},{4,5},{5,6},{6,7},{7,0},{8,9},{9,10},{10,1... | collective-permute-start | bytes 393224 | tf_op jit(solution)/shard_map/ppermute | solution.py:68
  44.2 5.0 %copy-start.2 = (bf16[128,512]{1,0:T(8,128)(2,1)S(1)}, bf16[128,512]{1,0:T(8,128)(2,1)}, u32[]{:S(2)}) copy-start(bf16[128,512]{1,0:T(8,128)(2,1)} %param.8) | copy-start | bytes 393220
  49.4 1.3 copy-start.1
  186.3 27.9 %all-to-all-start = ((bf16[64,4,512]{2,1,0:T(4,128)(2,1)}), bf16[64,4,512]{2,1,0:T(4,128)(2,1)S(1)}, u32[]{:S(2)}, u32[]{:S(2)}) async-start(bf16[64,4,512]{2,1,0:T(4,128)(2,1)} %broadcast_select_fusion), calls=%async_computation | async-start | bytes 524288 | tf_op jit(solution)/shard_map/all_to_all | solution.py:132
  220.2 19.6 %all-to-all-start.1 = ((bf16[64,4,4]{1,2,0:T(4,128)(2,1)}), bf16[64,4,4]{1,2,0:T(4,128)(2,1)S(1)}, u32[]{:S(2)}, u32[]{:S(2)}) async-start(bf16[64,4,4]{1,2,0:T(4,128)(2,1)} %copy.123), calls=%async_computation.1 | async-start | bytes 131072 | tf_op jit(solution)/shard_map/all_to_all | solution.py:149
  239.8 23.7 %all-to-all-start.2 = ((bf16[64,4,512]{2,1,0:T(4,128)(2,1)}), bf16[64,4,512]{2,1,0:T(4,128)(2,1)S(1)}, u32[]{:S(2)}, u32[]{:S(2)}) async-start(bf16[64,4,512]{2,1,0:T(4,128)(2,1)} %convert_element_type.91), calls=%async_computation.2 | async-start | bytes 524288 | tf_op jit(solution)/shard_map/all_to_all | solution.py:148
  245.5 54.3 %reduce-scatter.2.cloned.1.call-start = ((), (), s32[]{:S(2)}) async-start(), calls=%async_computation.5 | async-start | bytes 1179648 | tf_op jit(solution)/shard_map/reduce_scatter | solution.py:185
Sparse Core Ops, SparseCore 0:
  11.0 166.1 all-gather.1
  269.4 30.4 reduce-scatter.1
